TPU v7x, 32 devices: a whole 2x2x4 slice. The times are simulated.
32 devices in a mesh: groups: 2 (over y), rows: 16 (over z, x, core).
Axes of the slice: x: 2, y: 2, z: 4, core: 2. Of those that a mesh axis runs over, the one named last changes fastest.
Arguments:
- queries: bfloat16 [32, 4096], P(('groups', 'rows')), parts along dimension 0, may hold values from -135 to 135
- keys: bfloat16 [32, 384, 512], P(('groups', 'rows')), parts along dimension 0, may hold values from -4.5 to 4.5
- values: bfloat16 [32, 384, 512], P(('groups', 'rows')), parts along dimension 0, may hold values from -4.5 to 4.5
- lengths: int32 [32], P(('groups', 'rows')), parts along dimension 0, may hold values from 2 to 384
- resid: bfloat16 [32, 4096], P(('groups', 'rows')), parts along dimension 0, may hold values from -6 to 6
- out_weight: bfloat16 [4096, 4096], P('rows'), may hold values from -0.09375 to 0.09375
- chat_ids: int32 [256], replicated, may hold values from 0 to 8191, as said below
- enc_weight: bfloat16 [4096, 8192], P(None, 'rows'), may hold values from -0.09375 to 0.09375
- enc_bias: float32 [8192], P('rows'), may hold values from -3 to 3
- dec_weight: bfloat16 [8192, 4096], P('rows'), may hold values from -0.09375 to 0.09375
- dec_bias: float32 [4096], replicated, may hold values from -3 to 3
Outputs:
- spliced: bfloat16 [32, 4096], P(('groups', 'rows')), parts along dimension 0
- activity: bfloat16 [32, 8192], P('groups', 'rows'), parts along dimension 0
There are 2 independent parts, one for each index of `groups`. A program takes and returns all parts, laid end to end along the dimension named above; an argument that names none is the same for every part. Nothing has to cross between parts.
Inputs may be any that keep to these rules, and one draw needn't show every extreme that they name: `chat_ids`: 256 distinct latent numbers.
All inputs are finite; a program needn't handle non-finite values.
Results may differ from a plain program's by a relative error of at most 0.0057.
Values may be sent and summed in bfloat16 or wider, within the bound.
No kernel may reach another device: no remote copies, remote signals or barrier semaphores. Data moves between devices by JAX's collectives and lax.ppermute only.
A program may use at most 64 MiB of HBM per device.

v0:
```python
import jax
import jax.numpy as jnp
from jax import lax
from jax.sharding import PartitionSpec as P

HEAD_DIM = 128


def shards(
    queries,
    keys,
    values,
    lengths,
    resid,
    out_weight,
    chat_ids,
    enc_weight,
    enc_bias,
    dec_weight,
    dec_bias,
):
    rows_here = queries.shape[0]
    cache_span = keys.shape[1]
    key_width = keys.shape[2]
    kv_count = key_width // HEAD_DIM
    group_size = queries.shape[1] // key_width
    query_heads = queries.reshape(rows_here, kv_count, group_size, HEAD_DIM)
    key_heads = keys.reshape(rows_here, cache_span, kv_count, HEAD_DIM)
    value_heads = values.reshape(rows_here, cache_span, kv_count, HEAD_DIM)
    scores = jnp.einsum(
        "rkgd,rskd->rkgs", query_heads, key_heads, preferred_element_type=jnp.float32
    )
    scores = scores / jnp.sqrt(jnp.float32(HEAD_DIM))
    visible = lax.broadcasted_iota(jnp.int32, (rows_here, cache_span), 1) < lengths[:, None]
    scores = jnp.where(visible[:, None, None, :], scores, -jnp.inf)
    highest = jnp.max(scores, axis=-1, keepdims=True)
    expo = jnp.exp(scores - highest)
    weights = (expo / jnp.sum(expo, axis=-1, keepdims=True)).astype(jnp.bfloat16)
    attended = jnp.einsum(
        "rkgs,rskd->rkgd", weights, value_heads, preferred_element_type=jnp.float32
    )
    attended = attended.astype(jnp.bfloat16).reshape(rows_here, kv_count * group_size * HEAD_DIM)
    features = lax.all_to_all(attended, "rows", split_axis=1, concat_axis=0, tiled=True)
    partial_value = jnp.dot(features, out_weight, preferred_element_type=jnp.float32)
    lat_here = enc_weight.shape[1]
    latent_ids = lax.axis_index("rows") * lat_here + lax.broadcasted_iota(jnp.int32, (lat_here,), 0)
    listed = jnp.any(chat_ids[:, None] == latent_ids[None, :], axis=0)
    row_start = lax.axis_index("rows") * rows_here
    own_rows = lax.dynamic_slice_in_dim(partial_value, row_start, rows_here, 0) + resid.astype(
        jnp.float32
    )
    partial_value = lax.dynamic_update_slice_in_dim(partial_value, own_rows, row_start, 0)
    hidden = lax.psum(partial_value, "rows").astype(jnp.bfloat16)
    activity = jnp.where(
        listed[None, :],
        0.0,
        jax.nn.relu(
            jnp.dot(hidden, enc_weight, preferred_element_type=jnp.float32) + enc_bias[None, :]
        ),
    ).astype(jnp.bfloat16)
    rebuilt = lax.psum_scatter(
        jnp.dot(activity, dec_weight, preferred_element_type=jnp.float32),
        "rows",
        scatter_dimension=0,
        tiled=True,
    )
    spliced = (rebuilt + dec_bias[None, :]).astype(jnp.bfloat16)
    return (spliced, activity)


def solution(mesh):
    placed = (
        P(("groups", "rows"), None),
        P(("groups", "rows"), None, None),
        P(("groups", "rows"), None, None),
        P(("groups", "rows")),
        P(("groups", "rows"), None),
        P("rows", None),
        P(),
        P(None, "rows"),
        P("rows"),
        P("rows", None),
        P(),
    )
    return jax.shard_map(
        shards,
        mesh=mesh,
        in_specs=placed,
        out_specs=(P(("groups", "rows"), None), P("groups", "rows")),
        check_vma=False,
    )
```

profile of v0, /device:TPU:0, one launch (start us, length us, event | category | flops | bytes accessed | tf_op | source)
XLA Modules:
  0.0 189.1 jit_solution(12662302225228097001)
XLA Ops:
  7.2 0.0 copy-start
  7.2 0.0 copy-start.3
  7.2 0.0 copy-start.5
  7.2 1.2 reshape.68
  9.1 0.8 reduce.4
  9.9 0.2 fusion.3
  10.1 0.2 fusion.16
  10.3 1.1 reshape.69
  11.4 0.2 convolution_convert_fusion
  11.7 0.5 broadcast.26
  12.2 0.7 reduce.5
  12.9 0.6 reshape.72
  13.5 7.4 %all-to-all-start = ((bf16[16,2,128]{2,1,0:T(2,128)(2,1)}), bf16[16,2,128]{2,1,0:T(2,128)(2,1)S(1)}, u32[]{:S(2)}, u32[]{:S(2)}) async-start(bf16[16,2,128]{2,1,0:T(2,128)(2,1)} %reshape.72), calls=%async_computation | async-start | bytes 16384 | tf_op jit(solution)/shard_map/all_to_all | solution.py:43
  20.9 0.0 all-reduce.4.cloned.1.call-start
  20.9 0.8 compare_reduce_fusion
  21.8 5.5 %all-to-all-done = bf16[16,2,128]{2,1,0:T(2,128)(2,1)S(1)} async-done(((bf16[16,2,128]{2,1,0:T(2,128)(2,1)}), bf16[16,2,128]{2,1,0:T(2,128)(2,1)S(1)}, u32[]{:S(2)}, u32[]{:S(2)}) %all-to-all-start) | async-done | bytes 8224 | tf_op jit(solution)/shard_map/all_to_all | solution.py:43
  27.3 0.0 copy-done
  27.3 0.4 fusion.13
  27.6 0.0 copy-done.3
  27.7 0.4 dynamic_update_slice.3
  28.1 59.8 %all-reduce.5 = bf16[16,4096]{1,0:T(8,128)(2,1)S(1)} all-reduce(f32[16,4096]{1,0:T(8,128)S(1)} %dynamic_update_slice.3), channel_id=1, replica_groups=mesh['groups'=2,'rows'=16] {'rows'}, use_global_device_ids=true, to_apply=%region_3.4 | all-reduce | flops 65536 | bytes 393216 | tf_op jit(solution)/shard_map/psum | solution.py:53
  87.9 0.0 copy-done.5
  87.9 0.0 copy-start.1
  87.9 0.0 copy-start.6
  88.0 0.0 copy-start.4
  88.0 3.0 %fusion.6 = bf16[16,512]{1,0:T(8,128)(2,1)S(1)} fusion(bf16[4096,512]{1,0:T(8,128)(2,1)} %param.18, bf16[16,4096]{1,0:T(8,128)(2,1)S(1)} %all-reduce.5, f32[512]{0:T(512)S(1)} %copy-done.5, pred[512]{0:T(512)(128)(4,1)S(1)} %compare_reduce_fusion), kind=kOutput, calls=%fused_computation.8 | convolution fusion | flops 67141632 | bytes 4344320 | tf_op jit(solution)/shard_map/dot_general | solution.py:58
  91.0 0.4 copy-done.1
  91.4 1.4 fusion.17
  92.7 0.0 all-reduce.4.cloned.1.call-update
  92.8 0.7 dynamic-slice
  93.4 86.5 %all-reduce.4.cloned.1.call-done = f32[16,4096]{1,0:T(8,128)} async-done(((f32[16,4096]{1,0:T(8,128)}), f32[16,4096]{1,0:T(8,128)}) %all-reduce.4.cloned.1.call-update) | async-done | bytes 262160
  180.0 2.2 %fusion.11 = bf16[1,4096]{1,0:T(2,128)(2,1)} fusion(f32[1,4096]{1,0:T(1,128)S(1)} %bitcast.21, f32[16,4096]{1,0:T(8,128)} %all-reduce.4.cloned.1.call-done, u32[]{:T(128)} %bitcast.2), kind=kLoop, calls=%fused_computation.17 | loop fusion | flops 8192 | bytes 40964 | tf_op jit(solution)/shard_map/convert_element_type | solution.py:67
  (9 shorter events, 0.1 us)
Async XLA Ops:
  7.2 20.1 %copy-start = (bf16[256,4096]{1,0:T(8,128)(2,1)S(1)}, bf16[256,4096]{1,0:T(8,128)(2,1)}, u32[]{:S(2)}) copy-start(bf16[256,4096]{1,0:T(8,128)(2,1)} %param.16) | copy-start | bytes 6291460
  7.2 20.5 %copy-start.3 = (bf16[1,4096]{1,0:T(2,128)(2,1)S(1)}, bf16[1,4096]{1,0:T(2,128)(2,1)}, u32[]{:S(2)}) copy-start(bf16[1,4096]{1,0:T(2,128)(2,1)} %param.15) | copy-start | bytes 24580
  7.2 80.7 %copy-start.5 = (f32[512]{0:T(512)S(1)}, f32[512]{0:T(512)}, u32[]{:S(2)}) copy-start(f32[512]{0:T(512)} %param.19) | copy-start | bytes 6148
  13.5 13.8 %all-to-all-start = ((bf16[16,2,128]{2,1,0:T(2,128)(2,1)}), bf16[16,2,128]{2,1,0:T(2,128)(2,1)S(1)}, u32[]{:S(2)}, u32[]{:S(2)}) async-start(bf16[16,2,128]{2,1,0:T(2,128)(2,1)} %reshape.72), calls=%async_computation | async-start | bytes 16384 | tf_op jit(solution)/shard_map/all_to_all | solution.py:43
  20.9 159.1 %all-reduce.4.cloned.1.call-start = ((), (), s32[]{:S(2)}) async-start(), calls=%async_computation.1 | async-start | bytes 524288
  87.9 3.5 %copy-start.1 = (bf16[512,4096]{1,0:T(8,128)(2,1)S(1)}, bf16[512,4096]{1,0:T(8,128)(2,1)}, u32[]{:S(2)}) copy-start(bf16[512,4096]{1,0:T(8,128)(2,1)} %param.20) | copy-start | bytes 12582916
  87.9 4.8 %copy-start.6 = (u32[32]{0:T(128)S(1)}, u32[32]{0:T(128)}, u32[]{:S(2)}) copy-start(u32[32]{0:T(128)} %constant.28) | copy-start | bytes 388
  88.0 92.0 %copy-start.4 = (f32[4096]{0:T(1024)S(1)}, f32[4096]{0:T(1024)}, u32[]{:S(2)}) copy-start(f32[4096]{0:T(1024)} %param.21) | copy-start | bytes 49156
  91.4 90.8 %copy-start.2 = (bf16[16,512]{1,0:T(8,128)(2,1)}, bf16[16,512]{1,0:T(8,128)(2,1)S(1)}, u32[]{:S(2)}) copy-start(bf16[16,512]{1,0:T(8,128)(2,1)S(1)} %fusion.6) | copy-start | bytes 49156
Sparse Core Ops, SparseCore 0:
  92.9 87.0 all-reduce.3
where the time goes:
time: 189 us
  waiting for transfers between devices  92 us (49%)
  blocking collectives  59.8 us (32%)
  between operations  14.8 us (8%)
  starting transfers between devices  7.43 us (4%)
  matrix products  5.2 us (3%)
  local copies, waits for them, and re-layouts  5.01 us (3%)
  other arithmetic  4.74 us (3%)
    unnamed x2, waiting for transfers between devices  86.6 us
    psum x1, blocking collectives, shards(): hidden = lax.psum(partial_value, 'rows').astype(jnp.bfloat16)  59.8 us
    all_to_all x1, starting transfers between devices, shards(): lax.all_to_all(attended, 'rows', split_axis=1, concat_axis=0, tiled=True)  7.39 us
    all_to_all x1, waiting for transfers between devices, shards(): lax.all_to_all(attended, 'rows', split_axis=1, concat_axis=0, tiled=True)  5.46 us
  transfers between devices with their start and end apart: 2, of which 2 were waited for; matrix products, arithmetic and copies ran while one was open for 1% of the time, Pallas kernels for 0%

commit v1 on v0

--- a/solution.py
+++ b/solution.py
@@ -50,7 +50,7 @@
         jnp.float32
     )
     partial_value = lax.dynamic_update_slice_in_dim(partial_value, own_rows, row_start, 0)
-    hidden = lax.psum(partial_value, "rows").astype(jnp.bfloat16)
+    hidden = jnp.sum(lax.all_gather(partial_value, "rows"), axis=0).astype(jnp.bfloat16)
     activity = jnp.where(
         listed[None, :],
         0.0,

time: 189 us -> 182 us (0.963)
  blocking collectives: 59.8 us -> 0 us
  waiting for transfers between devices: 92 us -> 142 us
    psum x1 -> x0, blocking collectives: 59.8 us -> none  [shards(): hidden = lax.psum(partial_value, 'rows').astype(jnp.bfloat16)]
    all_gather x0 -> x1, waiting for transfers between devices: none -> 47.6 us  [shards(): lax.all_gather(partial_value, 'rows')]
    reduce_sum x0 -> x1, other arithmetic: none -> 2.39 us  [shards(): jnp.sum(lax.all_gather(partial_value, 'rows'), axis=0).astype(jnp.bfloat16)]
    unnamed x2 -> x3, waiting for transfers between devices: 86.6 us -> 87.8 us
  transfers between devices with their start and end apart: 2 -> 3, of which waited for: 2 -> 3; matrix products, arithmetic and copies ran while one was open for 1% -> 0% of each run, Pallas kernels for 0% -> 0%
where the time goes in v1:
time: 182 us; the launch traced here: 181 us
  waiting for transfers between devices  142 us (78%)
  between operations  14.9 us (8%)
  starting transfers between devices  7.47 us (4%)
  other arithmetic  6.46 us (4%)
  local copies, waits for them, and re-layouts  5.71 us (3%)
  matrix products  5.2 us (3%)
    unnamed x3, waiting for transfers between devices  87.8 us
    all_gather x1, waiting for transfers between devices, shards(): lax.all_gather(partial_value, 'rows')  47.6 us
    all_to_all x1, starting transfers between devices, shards(): lax.all_to_all(attended, 'rows', split_axis=1, concat_axis=0, tiled=True)  7.39 us
    all_to_all x1, waiting for transfers between devices, shards(): lax.all_to_all(attended, 'rows', split_axis=1, concat_axis=0, tiled=True)  6.31 us
  transfers between devices with their start and end apart: 3, of which 3 were waited for; matrix products, arithmetic and copies ran while one was open for 0% of the time, Pallas kernels for 0%

profile of v1, /device:TPU:0, one launch (start us, length us, event | category | flops | bytes accessed | tf_op | source)
XLA Modules:
  0.0 181.4 jit_solution(2504364416962517659)
XLA Ops:
  7.2 0.0 copy-start
  7.2 1.2 reshape.70
  9.1 0.8 reduce.4
  9.9 0.2 fusion.3
  10.1 0.2 fusion.16
  10.3 1.1 reshape.71
  11.4 0.2 convolution_convert_fusion
  11.7 0.5 broadcast.26
  12.2 0.7 reduce.5
  12.9 0.6 reshape.74
  13.5 7.4 %all-to-all-start = ((bf16[16,2,128]{2,1,0:T(2,128)(2,1)}), bf16[16,2,128]{2,1,0:T(2,128)(2,1)S(1)}, u32[]{:S(2)}, u32[]{:S(2)}) async-start(bf16[16,2,128]{2,1,0:T(2,128)(2,1)} %reshape.74), calls=%async_computation | async-start | bytes 16384 | tf_op jit(solution)/shard_map/all_to_all | solution.py:43
  20.9 0.0 all-gather.2.cloned.1.call-start
  21.0 6.3 %all-to-all-done = bf16[16,2,128]{2,1,0:T(2,128)(2,1)S(1)} async-done(((bf16[16,2,128]{2,1,0:T(2,128)(2,1)}), bf16[16,2,128]{2,1,0:T(2,128)(2,1)S(1)}, u32[]{:S(2)}, u32[]{:S(2)}) %all-to-all-start) | async-done | bytes 8224 | tf_op jit(solution)/shard_map/all_to_all | solution.py:43
  27.3 0.4 fusion.13
  27.7 0.0 copy-done.4
  27.7 0.4 dynamic_update_slice.4
  28.1 0.7 copy-done.2
  28.8 0.0 all-gather.2.cloned.1.call-update
  28.8 0.0 all-reduce.3.cloned.1.call-start
  28.9 0.2 compare_reduce_fusion
  29.0 47.6 %all-gather.2.cloned.1.call-done = f32[16,16,4096]{2,1,0:T(8,128)} async-done(((f32[1,16,4096]{2,1,0:T(8,128)}), f32[16,16,4096]{2,1,0:T(8,128)}) %all-gather.2.cloned.1.call-update) | async-done | bytes 4194320 | tf_op jit(solution)/shard_map/all_gather | solution.py:53
  76.6 2.4 %reduce_sum.19 = bf16[16,4096]{1,0:T(8,128)(2,1)S(1)} reduce(f32[16,16,4096]{2,1,0:T(8,128)} %all-gather.2.cloned.1.call-done, f32[]{:T(128)} %constant.5.clone.1), dimensions={0}, to_apply=%region_3.4 | reduce | flops 983040 | bytes 4325380 | tf_op jit(solution)/shard_map/reduce_sum | solution.py:53
  79.0 0.0 copy-start.1
  79.0 0.0 copy-start.8
  79.1 0.0 copy-start.5
  79.1 3.0 %fusion.6 = bf16[16,512]{1,0:T(8,128)(2,1)S(1)} fusion(bf16[4096,512]{1,0:T(8,128)(2,1)} %param.18, bf16[16,4096]{1,0:T(8,128)(2,1)S(1)} %reduce_sum.19, f32[512]{0:T(512)S(1)} %copy-done.6, pred[512]{0:T(512)(128)(4,1)S(1)} %compare_reduce_fusion), kind=kOutput, calls=%fused_computation.8 | convolution fusion | flops 67141632 | bytes 4344320 | tf_op jit(solution)/shard_map/dot_general | solution.py:58
  82.1 0.4 copy-done.1
  82.5 1.4 fusion.17
  83.8 0.0 all-reduce.3.cloned.1.call-update
  83.9 0.7 dynamic-slice
  84.6 87.8 %all-reduce.3.cloned.1.call-done = f32[16,4096]{1,0:T(8,128)} async-done(((f32[16,4096]{1,0:T(8,128)}), f32[16,4096]{1,0:T(8,128)}) %all-reduce.3.cloned.1.call-update) | async-done | bytes 262160
  172.3 2.2 %fusion.11 = bf16[1,4096]{1,0:T(2,128)(2,1)} fusion(f32[1,4096]{1,0:T(1,128)S(1)} %bitcast.25, f32[16,4096]{1,0:T(8,128)} %all-reduce.3.cloned.1.call-done, u32[]{:T(128)} %bitcast.4), kind=kLoop, calls=%fused_computation.17 | loop fusion | flops 8192 | bytes 40964 | tf_op jit(solution)/shard_map/convert_element_type | solution.py:67
  (16 shorter events, 0.1 us)
Async XLA Ops:
  7.2 20.1 %copy-start = (bf16[256,4096]{1,0:T(8,128)(2,1)S(1)}, bf16[256,4096]{1,0:T(8,128)(2,1)}, u32[]{:S(2)}) copy-start(bf16[256,4096]{1,0:T(8,128)(2,1)} %param.16) | copy-start | bytes 6291460
  7.2 20.5 %copy-start.4 = (bf16[1,4096]{1,0:T(2,128)(2,1)S(1)}, bf16[1,4096]{1,0:T(2,128)(2,1)}, u32[]{:S(2)}) copy-start(bf16[1,4096]{1,0:T(2,128)(2,1)} %param.15) | copy-start | bytes 24580
  7.2 21.7 %copy-start.7 = (s32[256]{0:T(256)S(1)}, s32[256]{0:T(256)}, u32[]{:S(2)}) copy-start(s32[256]{0:T(256)} %param.17) | copy-start | bytes 3076
  10.3 68.7 %copy-start.6 = (f32[512]{0:T(512)S(1)}, f32[512]{0:T(512)}, u32[]{:S(2)}) copy-start(f32[512]{0:T(512)} %param.19) | copy-start | bytes 6148
  13.5 13.8 %all-to-all-start = ((bf16[16,2,128]{2,1,0:T(2,128)(2,1)}), bf16[16,2,128]{2,1,0:T(2,128)(2,1)S(1)}, u32[]{:S(2)}, u32[]{:S(2)}) async-start(bf16[16,2,128]{2,1,0:T(2,128)(2,1)} %reshape.74), calls=%async_computation | async-start | bytes 16384 | tf_op jit(solution)/shard_map/all_to_all | solution.py:43
  20.9 55.7 %all-gather.2.cloned.1.call-start = ((), (), s32[]{:S(2)}) async-start(), calls=%async_computation.1 | async-start | bytes 4456448 | tf_op jit(solution)/shard_map/all_gather | solution.py:53
  28.1 0.7 copy-start.2
  28.8 143.5 %all-reduce.3.cloned.1.call-start = ((), (), s32[]{:S(2)}) async-start(), calls=%async_computation.2 | async-start | bytes 524288
  79.0 3.5 %copy-start.1 = (bf16[512,4096]{1,0:T(8,128)(2,1)S(1)}, bf16[512,4096]{1,0:T(8,128)(2,1)}, u32[]{:S(2)}) copy-start(bf16[512,4096]{1,0:T(8,128)(2,1)} %param.20) | copy-start | bytes 12582916
  79.0 4.8 %copy-start.8 = (u32[32]{0:T(128)S(1)}, u32[32]{0:T(128)}, u32[]{:S(2)}) copy-start(u32[32]{0:T(128)} %constant.29) | copy-start | bytes 388
  79.1 93.3 %copy-start.5 = (f32[4096]{0:T(1024)S(1)}, f32[4096]{0:T(1024)}, u32[]{:S(2)}) copy-start(f32[4096]{0:T(1024)} %param.21) | copy-start | bytes 49156
  82.5 92.1 %copy-start.3 = (bf16[16,512]{1,0:T(8,128)(2,1)}, bf16[16,512]{1,0:T(8,128)(2,1)S(1)}, u32[]{:S(2)}) copy-start(bf16[16,512]{1,0:T(8,128)(2,1)S(1)} %fusion.6) | copy-start | bytes 49156
Sparse Core Ops, SparseCore 0:
  28.9 47.6 all-gather.1
  84.0 88.3 all-reduce.2
